TPU v7x, 128 devices: a whole 4x4x4 slice. The times are simulated.
128 devices in a mesh: dp: 8 (over z, core), ctx: 16 (over y, x).
Axes of the slice: x: 4, y: 4, z: 4, core: 2. Of those that a mesh axis runs over, the one named last changes fastest.
Arguments:
- ids: int32 [8, 4096, 8], P('dp', 'ctx'), may hold values from 0 to 1023
- tables: bfloat16 [8, 1024, 1024], P(None, 'dp', 'ctx'), may hold values from -2.09375 to 2.09375
- w_qkv: bfloat16 [1024, 3072], P('dp'), may hold values from -5 to 5
- w_out: bfloat16 [1024, 1024], P('dp'), may hold values from -0.1875 to 0.1875
- attn_gain: float32 [1024], replicated, may hold values from 0.1 to 1.9
- conv_gain: float32 [1024], replicated, may hold values from 0.1 to 1.9
- conv_kernel: float32 [31, 1024], replicated, may hold values from -1 to 1
- back_list: int32 [16, 2], replicated, may hold values from 0 to 17, as said below
- ahead_list: int32 [16, 1], replicated, may hold values from 1 to 17, as said below
- cotangent: bfloat16 [8, 4096, 1024], P('dp', 'ctx'), may hold values from -8 to 8
Outputs:
- block_out: bfloat16 [8, 4096, 1024], P('dp', 'ctx')
- grad_embedded: bfloat16 [8, 4096, 1024], P('dp', 'ctx')
- grad_qkv: float32 [1024, 3072], P('dp')
- grad_out: float32 [1024, 1024], P('dp')
- grad_kernel: float32 [31, 1024], replicated
Inputs may be any that keep to these rules, and one draw needn't show every extreme that they name: `back_list`: row b lists distinct blocks among b - 2 .. b - 1 that exist, first, then the filler 16 + 1; block 2 and the last block list all 2, the first none. `ahead_list`: row b lists distinct blocks among b + 1 .. b + 1 that exist, first, then the filler 16 + 1; block 0 lists all 1, the last none.
All inputs are finite; a program needn't handle non-finite values.
Results may differ from a plain program's by a relative error of at most 0.015.
Values may be sent and summed in bfloat16 or wider, within the bound.
No kernel may reach another device: no remote copies, remote signals or barrier semaphores. Data moves between devices by JAX's collectives and lax.ppermute only.
A program may use at most 128 MiB of HBM per device.

v0:
```python
import jax
import jax.numpy as jnp
from jax import lax
from jax.sharding import PartitionSpec as P

HEADS = 16
EPSILON = 1e-06
NEGATIVE = -1e30


def from_behind(value, axis, steps):
    count = lax.axis_size(axis)
    first, last = (max(0, -steps), min(count, count - steps))
    return lax.ppermute(value, axis, [(source, source + steps) for source in range(first, last)])


def with_halo(block, sides, width):
    for axis, dim in sides:
        count = lax.axis_size(axis)
        forward = [(i, i + 1) for i in range(count - 1)]
        backward = [(target, source) for source, target in forward]
        low = lax.ppermute(
            lax.slice_in_dim(block, block.shape[dim] - width, None, axis=dim), axis, forward
        )
        high = lax.ppermute(lax.slice_in_dim(block, 0, width, axis=dim), axis, backward)
        block = jnp.concatenate([low, block, high], axis=dim)
    return block


def inverse_rms(features):
    return lax.rsqrt(jnp.mean(features * features, axis=-1, keepdims=True) + EPSILON)


def norm_back(features, inverse, gains, upstream):
    inner = jnp.mean(features * gains * upstream, axis=-1, keepdims=True)
    return inverse * gains * upstream - features * inverse * inverse * inverse * inner


def silu_slope(conv_sum):
    sigmoid = jax.nn.sigmoid(conv_sum)
    return sigmoid * (1.0 + conv_sum * (1.0 - sigmoid))


def block_scores(queries, key_block, listed_block, score_scale):
    return jnp.where(
        listed_block,
        jnp.einsum("rqhd,rkhd->rhqk", queries, key_block, preferred_element_type=jnp.float32)
        * score_scale,
        NEGATIVE,
    )


def probabilities(queries, key_part, listed, score_scale):
    pieces = [
        block_scores(queries, key_part[:, position], listed[position], score_scale)
        for position in range(key_part.shape[1])
    ]
    scores = jnp.concatenate(pieces, axis=3)
    highest = jnp.max(scores, axis=3, keepdims=True)
    weights = jnp.exp(scores - highest)
    return weights / jnp.sum(weights, axis=3, keepdims=True)


def on_device(
    ids, tables, w_qkv, w_out, attn_gain, conv_gain, conv_kernel, back_list, ahead_list, cotangent
):
    recordings = ids.shape[0]
    frames_dev = ids.shape[1]
    head_count = HEADS
    tap_count = conv_kernel.shape[0]
    rim_width = (tap_count - 1) // 2
    group_width = 4
    group_count = head_count // group_width
    ids_whole = lax.all_gather(ids, "ctx", axis=1, tiled=True)
    table_whole = lax.all_gather(tables, "dp", axis=1, tiled=True)
    columns = jnp.zeros(ids_whole.shape[:2] + (table_whole.shape[2],), jnp.float32)
    for codebook in range(table_whole.shape[0]):
        columns = columns + jnp.take(
            table_whole[codebook], ids_whole[:, :, codebook], axis=0
        ).astype(jnp.float32)
    embedded = lax.all_to_all(
        columns.astype(jnp.bfloat16), "ctx", split_axis=1, concat_axis=2, tiled=True
    )
    weight_qkv, weight_out = (
        lax.all_gather(w_qkv, "dp", axis=0, tiled=True),
        lax.all_gather(w_out, "dp", axis=0, tiled=True),
    )
    model_width = weight_out.shape[0]
    head_size = model_width // head_count
    score_scale = head_size ** (-0.5)
    features = embedded.astype(jnp.float32).reshape(-1, model_width)
    attn_inverse = inverse_rms(features)
    normed = (features * attn_inverse * attn_gain).astype(jnp.bfloat16)
    projected = jnp.dot(normed, weight_qkv, preferred_element_type=jnp.float32).astype(jnp.bfloat16)
    projected = projected.reshape(recordings, frames_dev, 3 * model_width)
    own_pairs = projected[:, :, model_width:]
    ctx_index = lax.axis_index("ctx")
    back_row = lax.dynamic_index_in_dim(back_list, ctx_index, 0, keepdims=False)
    ahead_row = lax.dynamic_index_in_dim(ahead_list, ctx_index, 0, keepdims=False)
    offsets = [-(step + 1) for step in range(back_list.shape[1])] + [1]
    listed_items = [jnp.array(True)]
    pair_blocks = [own_pairs]
    for offset in offsets:
        list_row = back_row if offset < 0 else ahead_row
        listed_items.append(jnp.any(list_row == ctx_index + offset))
        pair_blocks.append(from_behind(own_pairs, "ctx", -offset))
    listed = jnp.stack(listed_items)
    seen_count = len(pair_blocks)
    stacked = jnp.stack(pair_blocks, axis=1)
    key_all = stacked[..., :model_width].reshape(
        recordings, seen_count, frames_dev, head_count, head_size
    )
    value_all = stacked[..., model_width:].reshape(
        recordings, seen_count, frames_dev, head_count, head_size
    )
    query_all = projected[:, :, :model_width].reshape(recordings, frames_dev, head_count, head_size)

    def forward_group(group):
        first_head = group * group_width
        queries = lax.dynamic_slice_in_dim(query_all, first_head, group_width, 2)
        key_part = lax.dynamic_slice_in_dim(key_all, first_head, group_width, 3)
        value_part = lax.dynamic_slice_in_dim(value_all, first_head, group_width, 3)
        probs_low = probabilities(queries, key_part, listed, score_scale).astype(jnp.bfloat16)
        value_flat = value_part.reshape(recordings, -1, group_width, head_size)
        return jnp.einsum(
            "rhqk,rkhd->rqhd", probs_low, value_flat, preferred_element_type=jnp.float32
        ).astype(jnp.bfloat16)

    mixed = lax.map(forward_group, jnp.arange(group_count, dtype=jnp.int32))
    mixed = jnp.moveaxis(mixed, 0, 2).reshape(recordings * frames_dev, model_width)
    projection = jnp.dot(mixed, weight_out, preferred_element_type=jnp.float32)
    middle = (features + projection).astype(jnp.bfloat16)
    middle_wide = middle.astype(jnp.float32)
    conv_inverse = inverse_rms(middle_wide)
    conv_input = (
        (middle_wide * conv_inverse * conv_gain)
        .astype(jnp.bfloat16)
        .reshape(recordings, frames_dev, model_width)
    )
    padded = with_halo(conv_input, (("ctx", 1),), rim_width).astype(jnp.float32)
    conv_sum = jnp.zeros((recordings, frames_dev, model_width), jnp.float32)
    for tap_index in range(tap_count):
        conv_sum = conv_sum + conv_kernel[tap_index] * padded[:, tap_index : tap_index + frames_dev]
    middle_frames = middle_wide.reshape(recordings, frames_dev, model_width)
    block_out = (middle_frames + jax.nn.silu(conv_sum)).astype(jnp.bfloat16)
    upstream = cotangent.astype(jnp.float32)
    grad_conv_low = (upstream * silu_slope(conv_sum)).astype(jnp.bfloat16)
    grad_conv = lax.optimization_barrier(grad_conv_low).astype(jnp.float32)
    grad_padded = with_halo(grad_conv_low, (("ctx", 1),), rim_width).astype(jnp.float32)
    grad_input = jnp.zeros((recordings, frames_dev, model_width), jnp.float32)
    kernel_list = []
    for tap_index in range(tap_count):
        window = padded[:, tap_index : tap_index + frames_dev]
        kernel_list.append(jnp.sum(grad_conv * window, axis=(0, 1)))
        start_row = 2 * rim_width - tap_index
        grad_input = (
            grad_input + conv_kernel[tap_index] * grad_padded[:, start_row : start_row + frames_dev]
        )
    kernel_rows = jnp.stack(kernel_list)
    kernel_dp = lax.psum(kernel_rows, "dp")
    grad_middle = (
        upstream.reshape(-1, model_width)
        + norm_back(middle_wide, conv_inverse, conv_gain, grad_input.reshape(-1, model_width))
    ).astype(jnp.bfloat16)
    contract_rows = (((0,), (0,)), ((), ()))
    contract_columns = (((1,), (1,)), ((), ()))
    grad_mixed = lax.dot_general(
        grad_middle, weight_out, contract_columns, preferred_element_type=jnp.float32
    ).astype(jnp.bfloat16)
    mixed_columns = lax.all_to_all(mixed, "dp", split_axis=1, concat_axis=0, tiled=True)
    middle_rows = lax.all_gather(grad_middle, "dp", axis=0, tiled=True)
    grad_wout = lax.dot_general(
        mixed_columns, middle_rows, contract_rows, preferred_element_type=jnp.float32
    )
    grad_heads = grad_mixed.reshape(recordings, frames_dev, head_count, head_size)

    def backward_group(group):
        first_head = group * group_width
        queries = lax.dynamic_slice_in_dim(query_all, first_head, group_width, 2)
        key_part = lax.dynamic_slice_in_dim(key_all, first_head, group_width, 3)
        value_part = lax.dynamic_slice_in_dim(value_all, first_head, group_width, 3)
        grad_part = lax.dynamic_slice_in_dim(grad_heads, first_head, group_width, 2)
        probs = probabilities(queries, key_part, listed, score_scale)
        probs_low = probs.astype(jnp.bfloat16)
        key_flat = key_part.reshape(recordings, -1, group_width, head_size)
        value_flat = value_part.reshape(recordings, -1, group_width, head_size)
        grad_probs = jnp.einsum(
            "rqhd,rkhd->rhqk", grad_part, value_flat, preferred_element_type=jnp.float32
        )
        row_sum = jnp.sum(probs * grad_probs, axis=3, keepdims=True)
        grad_scores = (probs * (grad_probs - row_sum) * score_scale).astype(jnp.bfloat16)
        grad_query = jnp.einsum(
            "rhqk,rkhd->rqhd", grad_scores, key_flat, preferred_element_type=jnp.float32
        )
        grad_key = jnp.einsum(
            "rhqk,rqhd->rkhd", grad_scores, queries, preferred_element_type=jnp.float32
        )
        grad_value = jnp.einsum(
            "rhqk,rqhd->rkhd", probs_low, grad_part, preferred_element_type=jnp.float32
        )
        return (grad_query, grad_key, grad_value)

    grad_query, grad_key, grad_value = lax.map(
        backward_group, jnp.arange(group_count, dtype=jnp.int32)
    )
    grad_query = jnp.moveaxis(grad_query, 0, 2).reshape(recordings * frames_dev, model_width)
    grad_key = jnp.moveaxis(grad_key, 0, 2).reshape(recordings, seen_count, frames_dev, model_width)
    grad_value = jnp.moveaxis(grad_value, 0, 2).reshape(
        recordings, seen_count, frames_dev, model_width
    )
    pair_total = jnp.concatenate([grad_key[:, 0], grad_value[:, 0]], axis=2)
    for position, offset in enumerate(offsets):
        outgoing = jnp.concatenate(
            [grad_key[:, position + 1], grad_value[:, position + 1]], axis=2
        ).astype(jnp.bfloat16)
        arrived = from_behind(outgoing, "ctx", offset)
        pair_total = pair_total + arrived.astype(jnp.float32)
    grad_projected = jnp.concatenate(
        [
            grad_query.astype(jnp.bfloat16),
            pair_total.reshape(recordings * frames_dev, 2 * model_width).astype(jnp.bfloat16),
        ],
        axis=1,
    )
    normed_columns = lax.all_to_all(normed, "dp", split_axis=1, concat_axis=0, tiled=True)
    projected_rows = lax.all_gather(grad_projected, "dp", axis=0, tiled=True)
    grad_wqkv = lax.dot_general(
        normed_columns, projected_rows, contract_rows, preferred_element_type=jnp.float32
    )
    grad_normed = lax.dot_general(
        grad_projected, weight_qkv, contract_columns, preferred_element_type=jnp.float32
    )
    grad_embedded = (
        grad_middle.astype(jnp.float32) + norm_back(features, attn_inverse, attn_gain, grad_normed)
    ).astype(jnp.bfloat16)
    row_width = grad_wqkv.shape[1] + grad_wout.shape[1]
    kernel_padded = jnp.pad(
        kernel_dp, ((0, -tap_count * model_width % row_width // model_width), (0, 0))
    )
    kernel_packed = kernel_padded.reshape(-1, row_width)
    packed = jnp.concatenate(
        [jnp.concatenate([grad_wqkv, grad_wout], axis=1), kernel_packed], axis=0
    )
    summed = lax.psum(packed, "ctx")
    shard_rows = grad_wqkv.shape[0]
    grad_qkv = summed[:shard_rows, : grad_wqkv.shape[1]]
    grad_out = summed[:shard_rows, grad_wqkv.shape[1] :]
    grad_kernel = summed[shard_rows:].reshape(-1, model_width)[:tap_count]
    return (
        block_out,
        grad_embedded.reshape(recordings, frames_dev, model_width),
        grad_qkv,
        grad_out,
        grad_kernel,
    )


def solution(mesh):
    in_specs = (
        P("dp", "ctx", None),
        P(None, "dp", "ctx"),
        P("dp", None),
        P("dp", None),
        P(),
        P(),
        P(),
        P(),
        P(),
        P("dp", "ctx", None),
    )
    out_specs = (P("dp", "ctx", None), P("dp", "ctx", None), P("dp", None), P("dp", None), P())
    return jax.shard_map(
        on_device, mesh=mesh, in_specs=in_specs, out_specs=out_specs, check_vma=False
    )
```

profile of v0, /device:TPU:0, one launch (start us, length us, event | category | flops | bytes accessed | tf_op | source)
XLA Modules:
  0.0 895.1 jit_solution(8023950666195141221)
XLA Ops:
  9.8 24.0 %all_gather.19 = s32[1,4096,8]{1,2,0:T(8,128)S(1)} all-gather(s32[1,256,8]{1,2,0:T(8,128)} %param.16), channel_id=1, replica_groups=mesh['dp'=8,'ctx'=16] {'ctx'}, dimensions={1}, use_global_device_ids=true | all-gather | bytes 139264 | tf_op jit(solution)/shard_map/all_gather | solution.py:74
  39.8 12.1 %gather_fusion = bf16[4096,64]{1,0:T(8,128)(2,1)S(1)} fusion(bf16[1024,64]{1,0:T(8,128)(2,1)S(1)} %get-tuple-element.450, s32[4096]{0:T(1024)S(1)} %broadcast_clamp_fusion.7), kind=kCustom, calls=%fused_computation.clone | custom fusion | bytes 1064960 | tf_op jit(solution)/shard_map/jit(_take)/gather | solution.py:78
  52.0 15.0 %gather_fusion.7 = bf16[4096,64]{1,0:T(8,128)(2,1)} fusion(bf16[1024,64]{1,0:T(8,128)(2,1)S(1)} %get-tuple-element.451, s32[4096]{0:T(1024)S(1)} %broadcast_clamp_fusion), kind=kCustom, calls=%fused_computation.7.clone | custom fusion | bytes 1064960 | tf_op jit(solution)/shard_map/jit(_take)/gather | solution.py:78
  67.0 14.9 %gather_fusion.6 = bf16[4096,64]{1,0:T(8,128)(2,1)} fusion(bf16[1024,64]{1,0:T(8,128)(2,1)S(1)} %get-tuple-element.452, s32[4096]{0:T(1024)S(1)} %broadcast_clamp_fusion.1), kind=kCustom, calls=%fused_computation.6.clone | custom fusion | bytes 1064960 | tf_op jit(solution)/shard_map/jit(_take)/gather | solution.py:78
  81.9 14.9 %gather_fusion.5 = bf16[4096,64]{1,0:T(8,128)(2,1)} fusion(bf16[1024,64]{1,0:T(8,128)(2,1)S(1)} %get-tuple-element.453, s32[4096]{0:T(1024)S(1)} %broadcast_clamp_fusion.2), kind=kCustom, calls=%fused_computation.5.clone | custom fusion | bytes 1064960 | tf_op jit(solution)/shard_map/jit(_take)/gather | solution.py:78
  96.8 14.9 %gather_fusion.4 = bf16[4096,64]{1,0:T(8,128)(2,1)} fusion(bf16[1024,64]{1,0:T(8,128)(2,1)S(1)} %get-tuple-element.454, s32[4096]{0:T(1024)S(1)} %broadcast_clamp_fusion.3), kind=kCustom, calls=%fused_computation.4.clone | custom fusion | bytes 1064960 | tf_op jit(solution)/shard_map/jit(_take)/gather | solution.py:78
  111.7 14.9 %gather_fusion.3 = bf16[4096,64]{1,0:T(8,128)(2,1)} fusion(bf16[1024,64]{1,0:T(8,128)(2,1)S(1)} %get-tuple-element.455, s32[4096]{0:T(1024)S(1)} %broadcast_clamp_fusion.4), kind=kCustom, calls=%fused_computation.3.clone | custom fusion | bytes 1064960 | tf_op jit(solution)/shard_map/jit(_take)/gather | solution.py:78
  126.6 14.9 %gather_fusion.2 = bf16[4096,64]{1,0:T(8,128)(2,1)} fusion(bf16[1024,64]{1,0:T(8,128)(2,1)S(1)} %get-tuple-element.456, s32[4096]{0:T(1024)S(1)} %broadcast_clamp_fusion.5), kind=kCustom, calls=%fused_computation.2.clone | custom fusion | bytes 1064960 | tf_op jit(solution)/shard_map/jit(_take)/gather | solution.py:78
  141.5 14.9 %gather_fusion.1 = bf16[4096,64]{1,0:T(8,128)(2,1)} fusion(bf16[1024,64]{1,0:T(8,128)(2,1)S(1)} %get-tuple-element.457, s32[4096]{0:T(1024)S(1)} %broadcast_clamp_fusion.6), kind=kCustom, calls=%fused_computation.1.clone | custom fusion | bytes 1064960 | tf_op jit(solution)/shard_map/jit(_take)/gather | solution.py:78
  156.4 8.9 add_convert_fusion
  165.4 16.7 %copy.339 = bf16[1,4096,64]{2,0,1:T(2,128)(2,1)S(1)} copy(bf16[1,4096,64]{2,1,0:T(8,128)(2,1)S(1)} %add_convert_fusion) | data formatting | bytes 1048576 | tf_op jit(solution)/shard_map/convert_element_type | solution.py:82
  182.6 22.4 %reduce.51 = bf16[4096,64]{1,0:T(8,128)(2,1)S(1)} reduce(bf16[4096,1,64]{2,1,0:T(2,128)(2,1)S(1)} %bitcast.477, bf16[]{:T(256)} %broadcast.264), dimensions={1}, to_apply=%bitcast.392.reduce_sub_computation | reduce | bytes 1048578
  205.8 18.8 %all_to_all.44 = bf16[16,2,8192]{2,1,0:T(2,128)(2,1)S(1)} all-to-all(bf16[16,2,8192]{2,1,0:T(2,128)(2,1)S(1)} %reshape.933), channel_id=1, replica_groups=mesh['dp'=8,'ctx'=16] {'ctx'}, dimensions={0} | all-to-all | bytes 1048576 | tf_op jit(solution)/shard_map/all_to_all | solution.py:81
  230.3 4.6 fusion.102
  249.1 13.9 %collective-permute-done.1 = bf16[1,256,2048]{2,1,0:T(8,128)(2,1)} collective-permute-done((bf16[1,256,2048]{2,1,0:T(8,128)(2,1)}, bf16[1,256,2048]{2,1,0:T(8,128)(2,1)}, u32[]{:S(2)}, u32[]{:S(2)}) %collective-permute-start.1) | collective-permute-done | bytes 1048608 | tf_op jit(solution)/shard_map/ppermute | solution.py:14
  263.0 21.3 %collective-permute-done = bf16[1,256,2048]{2,1,0:T(8,128)(2,1)} collective-permute-done((bf16[1,256,2048]{2,1,0:T(8,128)(2,1)}, bf16[1,256,2048]{2,1,0:T(8,128)(2,1)}, u32[]{:S(2)}, u32[]{:S(2)}) %collective-permute-start) | collective-permute-done | bytes 1048608 | tf_op jit(solution)/shard_map/ppermute | solution.py:14
  288.9 4.0 copy.299
  292.8 3.9 copy.297
  296.7 4.8 copy.300
  301.5 46.3 %while.24 = (s32[]{:T(128)}, bf16[4,1,256,4,64]{2,4,3,1,0:T(8,128)(2,1)}, s32[4]{0:T(128)S(1)}, bf16[1,4,256,16,64]{2,1,4,3,0:T(4,128)(2,1)}, bf16[1,256,16,64]{...) while((s32[]{:T(128)}, ...), condition=%wide.region_10.12_spmd, body=%wide.region_4.11_spmd.sunk | while | flops 282916864 | bytes 16444675 | solution.py:129
  350.7 4.4 collective-permute-start.3
  357.0 4.0 collective-permute-done.4
  361.1 5.3 fusion.115
  378.3 5.6 fusion.120
  388.2 143.3 %while.25 = (s32[]{:T(128)}, bf16[4,1,256,4,64]{2,4,3,1,0:T(8,128)(2,1)}, f32[4,1,1024,4,64]{2,4,3,1,0:T(8,128)}, f32[4,1,1024,4,64]{2,4,3,1,0:T(8,128)}, s32[4]...) while((s32[]{:T(128)}, ...), condition=%wide.region_20.22_spmd, body=%wide.region_13.21_spmd.sunk | while | flops 716965888 | bytes 66809192 | solution.py:203
  406.4 7.0 fusion.265
  413.4 7.3 fusion.266
  442.0 7.0 fusion.265
  449.0 8.0 fusion.266
  478.4 7.0 fusion.265
  485.4 7.3 fusion.266
  514.0 7.0 fusion.265
  521.0 7.3 fusion.266
  531.4 5.6 reshape.813
  542.1 5.8 reshape.812
  550.8 3.8 fusion.198
  574.6 7.6 pad_maximum_fusion.2
  583.5 7.3 pad_maximum_fusion.3
  590.8 5.5 collective-permute-start.9
  596.3 4.9 slice_bitcast_fusion
  601.4 35.3 %collective-permute-done.8 = bf16[1,256,2048]{1,0,2:T(2,128)(2,1)S(1)} collective-permute-done((bf16[1,256,2048]{1,0,2:T(2,128)(2,1)S(1)}, bf16[1,256,2048]{1,0,2:T(2,128)(2,1)S(1)}, u32[]{:S(2)}, u32[]{:S(2)}) %collective-permute-start.8) | collective-permute-done | bytes 1048608 | tf_op jit(solution)/shard_map/ppermute | solution.py:14
  638.7 19.2 %fusion.105 = bf16[1,256,2048]{1,0,2:T(2,128)(2,1)S(1)} fusion(bf16[1,256,2048]{1,0,2:T(2,128)(2,1)S(1)} %collective-permute-done.9, bf16[1,256,2048]{1,0,2:T(2,128)(2,1)S(1)} %collective-permute-done.8, f32[1,256,2048]{1,2,0:T(8,128)S(1)} %convert_element_type.227, f32[1,256,1024]{1,0,2:T(1,128)S(1)} %get-tuple-element.513, ...), kind=kLoop, calls=%fused_computation.149 | loop fusion | flops 3670016 | bytes 7340032 | tf_op jit(solution)/shard_map/convert_element_type | solution.py:221
  659.7 13.6 %all_to_all.45 = bf16[256,8,128]{0,2,1:T(8,128)(2,1)S(1)} all-to-all(bf16[256,8,128]{0,2,1:T(8,128)(2,1)S(1)} %multiply_convert_fusion.1), channel_id=1, replica_groups=mesh['dp'=8,'ctx'=16] {'dp'}, dimensions={1} | all-to-all | bytes 1048576 | tf_op jit(solution)/shard_map/all_to_all | solution.py:225
  678.4 8.6 all-to-all-done.2
  690.3 83.4 %all-gather.12.cloned.1.call-done = bf16[2048,3072]{0,1:T(8,128)(2,1)} async-done(((bf16[256,3072]{0,1:T(8,128)(2,1)}), bf16[2048,3072]{0,1:T(8,128)(2,1)}) %all-gather.12.cloned.1.call-update) | async-done | bytes 12582928 | tf_op jit(solution)/shard_map/all_gather | solution.py:226
  773.7 8.9 fusion.203
  786.7 4.8 multiply_reduce_fusion.1
  792.7 88.8 %all-reduce.6.cloned.1.call-done = f32[136,4096]{1,0:T(8,128)} async-done(((f32[136,4096]{1,0:T(8,128)}), f32[136,4096]{1,0:T(8,128)}) %all-reduce.6.cloned.1.call-update) | async-done | bytes 2228240 | tf_op jit(solution)/shard_map/psum | solution.py:244
  (271 shorter events, 232.9 us)
Async XLA Ops:
  7.2 237.8 %copy-start = (s32[16,1]{0,1:T(1,128)S(1)}, s32[16,1]{0,1:T(1,128)}, u32[]{:S(2)}) copy-start(s32[16,1]{0,1:T(1,128)} %param.24) | copy-start | bytes 196
  7.2 31.0 %all-gather.6.cloned.1.call-start = ((), (), s32[]{:S(2)}) async-start(), calls=%async_computation.3 | async-start | bytes 2359296 | tf_op jit(solution)/shard_map/all_gather | solution.py:75
  9.0 220.7 %all-gather.8.cloned.1.call-start = ((), (), s32[]{:S(2)}) async-start(), calls=%async_computation.4 | async-start | bytes 7077888 | tf_op jit(solution)/shard_map/all_gather | solution.py:85
  9.8 338.1 %all-gather.10.cloned.1.call-start = ((), (), s32[]{:S(2)}) async-start(), calls=%async_computation.5 | async-start | bytes 2359296 | tf_op jit(solution)/shard_map/all_gather | solution.py:86
  141.5 14.9 %copy-start.12 = (bf16[4096,64]{1,0:T(8,128)(2,1)S(1)}, bf16[4096,64]{1,0:T(8,128)(2,1)}, u32[]{:S(2)}) copy-start(bf16[4096,64]{1,0:T(8,128)(2,1)} %gather_fusion.7) | copy-start | bytes 1572868
  228.1 2.2 copy-start.19
  229.2 5.7 copy-start.8
  229.6 118.3 %copy-start.6 = (f32[256,1024]{1,0:T(8,128)}, f32[256,1024]{1,0:T(8,128)S(1)}, u32[]{:S(2)}) copy-start(f32[256,1024]{1,0:T(8,128)S(1)} %copy.302) | copy-start | bytes 3145732
  229.6 0.6 copy-start.21
  229.6 16.6 %copy-start.23 = (s32[16,2]{0,1:T(2,128)S(1)}, s32[16,2]{0,1:T(2,128)}, u32[]{:S(2)}) copy-start(s32[16,2]{0,1:T(2,128)} %param.23) | copy-start | bytes 388
  229.7 17.3 %copy-start.17 = (f32[31,1024]{1,0:T(8,128)S(1)}, f32[31,1024]{1,0:T(8,128)}, u32[]{:S(2)}) copy-start(f32[31,1024]{1,0:T(8,128)} %param.22) | copy-start | bytes 380932
  234.9 1.5 copy-start.14
  236.4 26.6 %collective-permute-start.1 = (bf16[1,256,2048]{2,1,0:T(8,128)(2,1)}, bf16[1,256,2048]{2,1,0:T(8,128)(2,1)}, u32[]{:S(2)}, u32[]{:S(2)}) collective-permute-start(bf16[1,256,2048]{2,1,0:T(8,128)(2,1)} %get-tuple-element.459), channel_id=1, source_target_pairs={{0,2},{1,3},{2,4},{3,5},{4,6},{5,7},{6,8},{7,9},{8,10},{9,11},{10,... | collective-permute-start | bytes 3145736 | tf_op jit(solution)/shard_map/ppermute | solution.py:14
  240.1 44.2 %collective-permute-start = (bf16[1,256,2048]{2,1,0:T(8,128)(2,1)}, bf16[1,256,2048]{2,1,0:T(8,128)(2,1)}, u32[]{:S(2)}, u32[]{:S(2)}) collective-permute-start(bf16[1,256,2048]{2,1,0:T(8,128)(2,1)} %get-tuple-element.459), channel_id=1, source_target_pairs={{0,1},{1,2},{2,3},{3,4},{4,5},{5,6},{6,7},{7,8},{8,9},{9,10},{10,1... | collective-permute-start | bytes 3145736 | tf_op jit(solution)/shard_map/ppermute | solution.py:14
  243.6 40.7 %collective-permute-start.2 = (bf16[1,256,2048]{2,1,0:T(8,128)(2,1)}, bf16[1,256,2048]{2,1,0:T(8,128)(2,1)}, u32[]{:S(2)}, u32[]{:S(2)}) collective-permute-start(bf16[1,256,2048]{2,1,0:T(8,128)(2,1)} %get-tuple-element.459), channel_id=1, source_target_pairs={{1,0},{2,1},{3,2},{4,3},{5,4},{6,5},{7,6},{8,7},{9,8},{10,9},{11,1... | collective-permute-start | bytes 3145736 | tf_op jit(solution)/shard_map/ppermute | solution.py:14
  244.9 432.5 %all-reduce.4.cloned.1.call-start = ((), (), s32[]{:S(2)}) async-start(), calls=%async_computation.8 | async-start | bytes 262144 | tf_op jit(solution)/shard_map/psum | solution.py:160
  347.8 2.7 copy-start.18
  347.8 13.3 %copy-start.13 = (bf16[1,256,1024]{2,1,0:T(8,128)(2,1)S(1)}, bf16[1,256,1024]{2,1,0:T(8,128)(2,1)}, u32[]{:S(2)}) copy-start(bf16[1,256,1024]{2,1,0:T(8,128)(2,1)} %param.25) | copy-start | bytes 1572868
  350.5 33.4 %copy-start.4 = (bf16[256,1024]{1,0:T(8,128)(2,1)}, bf16[256,1024]{1,0:T(8,128)(2,1)S(1)}, u32[]{:S(2)}) copy-start(bf16[256,1024]{1,0:T(8,128)(2,1)S(1)} %get-tuple-element.510) | copy-start | bytes 1572868
  350.7 6.2 collective-permute-start.3
  355.2 5.8 collective-permute-start.4
  369.0 9.1 %collective-permute-start.5 = (bf16[1,15,1024]{2,1,0:T(8,128)(2,1)S(1)}, bf16[1,15,1024]{2,1,0:T(8,128)(2,1)S(1)}, u32[]{:S(2)}, u32[]{:S(2)}) collective-permute-start(bf16[1,15,1024]{2,1,0:T(8,128)(2,1)S(1)} %get-tuple-element.460), channel_id=1, source_target_pairs={{0,1},{1,2},{2,3},{3,4},{4,5},{5,6},{6,7},{7,8},{8,9},{9,10},{10,1... | collective-permute-start | bytes 92168 | tf_op jit(solution)/shard_map/ppermute | solution.py:22
  372.3 5.8 collective-permute-start.6
  378.1 309.3 %all-gather.14.cloned.1.call-start = ((), (), s32[]{:S(2)}) async-start(), calls=%async_computation.7 | async-start | bytes 4718592 | tf_op jit(solution)/shard_map/all_gather | solution.py:171
  384.4 3.6 copy-start.10
  388.0 385.7 %all-gather.12.cloned.1.call-start = ((), (), s32[]{:S(2)}) async-start(), calls=%async_computation.6 | async-start | bytes 14155776 | tf_op jit(solution)/shard_map/all_gather | solution.py:226
  396.4 6.3 copy-start.3
  401.1 1.0 copy-start.2
  432.1 6.3 copy-start.3
  436.8 1.0 copy-start.2
  468.4 6.3 copy-start.3
  473.1 1.0 copy-start.2
  504.1 6.3 copy-start.3
  508.8 1.0 copy-start.2
  573.3 27.9 %collective-permute-start.7 = (bf16[1,256,2048]{1,2,0:T(8,128)(2,1)S(1)}, bf16[1,256,2048]{1,2,0:T(8,128)(2,1)S(1)}, u32[]{:S(2)}, u32[]{:S(2)}) collective-permute-start(bf16[1,256,2048]{1,2,0:T(8,128)(2,1)S(1)} %pad_maximum_fusion.5), channel_id=1, source_target_pairs={{1,0},{2,1},{3,2},{4,3},{5,4},{6,5},{7,6},{8,7},{9,8},{10,9},{11,1... | collective-permute-start | bytes 3145736 | tf_op jit(solution)/shard_map/ppermute | solution.py:14
  582.2 54.5 %collective-permute-start.8 = (bf16[1,256,2048]{1,0,2:T(2,128)(2,1)S(1)}, bf16[1,256,2048]{1,0,2:T(2,128)(2,1)S(1)}, u32[]{:S(2)}, u32[]{:S(2)}) collective-permute-start(bf16[1,256,2048]{1,0,2:T(2,128)(2,1)S(1)} %pad_maximum_fusion.2), channel_id=1, source_target_pairs={{2,0},{3,1},{4,2},{5,3},{6,4},{7,5},{8,6},{9,7},{10,8},{11,9},{12,... | collective-permute-start | bytes 3145736 | tf_op jit(solution)/shard_map/ppermute | solution.py:14
  590.8 48.0 %collective-permute-start.9 = (bf16[1,256,2048]{1,0,2:T(2,128)(2,1)S(1)}, bf16[1,256,2048]{1,0,2:T(2,128)(2,1)S(1)}, u32[]{:S(2)}, u32[]{:S(2)}) collective-permute-start(bf16[1,256,2048]{1,0,2:T(2,128)(2,1)S(1)} %pad_maximum_fusion.3), channel_id=1, source_target_pairs={{0,1},{1,2},{2,3},{3,4},{4,5},{5,6},{6,7},{7,8},{8,9},{9,10},{10,1... | collective-permute-start | bytes 3145736 | tf_op jit(solution)/shard_map/ppermute | solution.py:14
  638.7 19.4 %copy-start.15 = (bf16[4,1,256,4,64]{2,4,3,1,0:T(8,128)(2,1)S(1)}, bf16[4,1,256,4,64]{2,4,3,1,0:T(8,128)(2,1)}, u32[]{:S(2)}) copy-start(bf16[4,1,256,4,64]{2,4,3,1,0:T(8,128)(2,1)} %get-tuple-element.118) | copy-start | bytes 1572868
  657.9 1.5 copy-start.9
  657.9 1.5 copy-start.20
  657.9 1.5 copy-start.22
  673.2 13.8 %all-to-all-start.2 = ((bf16[256,8,128]{0,2,1:T(8,128)(2,1)}), bf16[256,8,128]{0,2,1:T(8,128)(2,1)S(1)}, u32[]{:S(2)}, u32[]{:S(2)}) async-start(bf16[256,8,128]{0,2,1:T(8,128)(2,1)} %bitcast.135), calls=%async_computation.2 | async-start | bytes 1048576 | tf_op jit(solution)/shard_map/all_to_all | solution.py:170
  676.8 204.8 %all-reduce.6.cloned.1.call-start = ((), (), s32[]{:S(2)}) async-start(), calls=%async_computation.9 | async-start | bytes 4456448 | tf_op jit(solution)/shard_map/psum | solution.py:244
  782.6 1.6 copy-start.5
  782.7 4.0 copy-start.7
  784.2 2.5 copy-start.16
  786.7 4.8 copy-start.11
  786.7 101.0 %copy-start.1 = (s32[16,1]{0,1:T(1,128)S(1)}, s32[16,1]{0,1:T(1,128)}, u32[]{:S(2)}) copy-start(s32[16,1]{0,1:T(1,128)} %param.24) | copy-start | bytes 196
Sparse Core Ops, SparseCore 0:
  10.3 27.8 all-gather.5
  39.9 41.4 all-gather.7
  245.0 24.3 all-gather.9
  378.2 62.7 all-reduce.3
  442.6 31.2 all-gather.13
  659.6 114.0 all-gather.11
  784.4 97.1 all-reduce.5
where the time goes:
time: 906 us; the launch traced here: 895 us
  waiting for transfers between devices  262 us (29%)
  local copies, waits for them, and re-layouts  252 us (28%)
  matrix products  170 us (19%)
  other arithmetic  101 us (11%)
  blocking collectives  56.4 us (6%)
  starting transfers between devices  31.5 us (3%)
  between operations  16.1 us (2%)
    gather x8, local copies, waits for them, and re-layouts, on_device(): jnp.take(table_whole[codebook], ids_whole[:, :, codebook], axis=0)  117 us
    psum x1, waiting for transfers between devices, on_device(): summed = lax.psum(packed, 'ctx')  88.8 us
    all_gather x1, waiting for transfers between devices, on_device(): projected_rows = lax.all_gather(grad_projected, 'dp', axis=0, tiled=True)  83.4 us
    ppermute x6, waiting for transfers between devices, from_behind(): lax.ppermute(value, axis, [(source, source + steps) for source in range(f...  72.6 us
    dot_general x32, matrix products, block_scores(): jnp.einsum('rqhd,rkhd->rhqk', queries, key_block, preferred_element_type=...  52.1 us
    dot_general x4, matrix products, backward_group(): jnp.einsum('rhqk,rqhd->rkhd', grad_scores, queries, preferred_element_typ...  29.9 us
    dot_general x4, matrix products, backward_group(): jnp.einsum('rhqk,rkhd->rqhd', grad_scores, key_flat, preferred_element_ty...  28 us
    all_gather x1, blocking collectives, on_device(): ids_whole = lax.all_gather(ids, 'ctx', axis=1, tiled=True)  24 us
  transfers between devices with their start and end apart: 18, of which 9 were waited for; matrix products, arithmetic and copies ran while one was open for 54% of the time, Pallas kernels for 0%

commit v1 on v0

--- a/solution.py
+++ b/solution.py
@@ -241,7 +241,7 @@
     packed = jnp.concatenate(
         [jnp.concatenate([grad_wqkv, grad_wout], axis=1), kernel_packed], axis=0
     )
-    summed = lax.psum(packed, "ctx")
+    summed = jnp.sum(lax.all_gather(packed, "ctx"), axis=0)
     shard_rows = grad_wqkv.shape[0]
     grad_qkv = summed[:shard_rows, : grad_wqkv.shape[1]]
     grad_out = summed[:shard_rows, grad_wqkv.shape[1] :]

time: 906 us -> 1030 us (1.14)
  waiting for transfers between devices: 262 us -> 379 us
  other arithmetic: 101 us -> 114 us
    all_gather x0 -> x1, waiting for transfers between devices: none -> 206 us  [on_device(): summed = jnp.sum(lax.all_gather(packed, 'ctx'), axis=0)]
    psum x1 -> x0, waiting for transfers between devices: 88.8 us -> none  [on_device(): summed = lax.psum(packed, 'ctx')]
    reduce_sum x0 -> x1, other arithmetic: none -> 13.2 us  [on_device(): summed = jnp.sum(lax.all_gather(packed, 'ctx'), axis=0)]
  transfers between devices with their start and end apart: 18 -> 18, of which waited for: 9 -> 9; matrix products, arithmetic and copies ran while one was open for 54% -> 47% of each run, Pallas kernels for 0% -> 0%
where the time goes in v1:
time: 1030 us; the launch traced here: 1020 us
  waiting for transfers between devices  379 us (37%)
  local copies, waits for them, and re-layouts  249 us (24%)
  matrix products  171 us (17%)
  other arithmetic  114 us (11%)
  blocking collectives  56.3 us (5%)
  starting transfers between devices  31.5 us (3%)
  between operations  16.1 us (2%)
    all_gather x1, waiting for transfers between devices, on_device(): summed = jnp.sum(lax.all_gather(packed, 'ctx'), axis=0)  206 us
    gather x8, local copies, waits for them, and re-layouts, on_device(): jnp.take(table_whole[codebook], ids_whole[:, :, codebook], axis=0)  117 us
    all_gather x1, waiting for transfers between devices, on_device(): projected_rows = lax.all_gather(grad_projected, 'dp', axis=0, tiled=True)  83.3 us
    ppermute x6, waiting for transfers between devices, from_behind(): lax.ppermute(value, axis, [(source, source + steps) for source in range(f...  72.7 us
    dot_general x32, matrix products, block_scores(): jnp.einsum('rqhd,rkhd->rhqk', queries, key_block, preferred_element_type=...  52.2 us
    dot_general x4, matrix products, backward_group(): jnp.einsum('rhqk,rqhd->rkhd', grad_scores, queries, preferred_element_typ...  30.3 us
    dot_general x4, matrix products, backward_group(): jnp.einsum('rhqk,rkhd->rqhd', grad_scores, key_flat, preferred_element_ty...  28.4 us
    all_gather x1, blocking collectives, on_device(): ids_whole = lax.all_gather(ids, 'ctx', axis=1, tiled=True)  24 us
  transfers between devices with their start and end apart: 18, of which 9 were waited for; matrix products, arithmetic and copies ran while one was open for 47% of the time, Pallas kernels for 0%

profile of v1, /device:TPU:0, one launch (start us, length us, event | category | flops | bytes accessed | tf_op | source)
XLA Modules:
  0.0 1022.7 jit_solution(2993364734428720117)
XLA Ops:
  9.8 24.0 %all_gather.25 = s32[1,4096,8]{1,2,0:T(8,128)S(1)} all-gather(s32[1,256,8]{1,2,0:T(8,128)} %param.16), channel_id=1, replica_groups=mesh['dp'=8,'ctx'=16] {'ctx'}, dimensions={1}, use_global_device_ids=true | all-gather | bytes 139264 | tf_op jit(solution)/shard_map/all_gather | solution.py:74
  39.8 12.1 %gather_fusion = bf16[4096,64]{1,0:T(8,128)(2,1)S(1)} fusion(bf16[1024,64]{1,0:T(8,128)(2,1)S(1)} %get-tuple-element.450, s32[4096]{0:T(1024)S(1)} %broadcast_clamp_fusion.7), kind=kCustom, calls=%fused_computation.clone | custom fusion | bytes 1064960 | tf_op jit(solution)/shard_map/jit(_take)/gather | solution.py:78
  52.0 15.0 %gather_fusion.7 = bf16[4096,64]{1,0:T(8,128)(2,1)} fusion(bf16[1024,64]{1,0:T(8,128)(2,1)S(1)} %get-tuple-element.451, s32[4096]{0:T(1024)S(1)} %broadcast_clamp_fusion), kind=kCustom, calls=%fused_computation.7.clone | custom fusion | bytes 1064960 | tf_op jit(solution)/shard_map/jit(_take)/gather | solution.py:78
  67.0 14.9 %gather_fusion.6 = bf16[4096,64]{1,0:T(8,128)(2,1)} fusion(bf16[1024,64]{1,0:T(8,128)(2,1)S(1)} %get-tuple-element.452, s32[4096]{0:T(1024)S(1)} %broadcast_clamp_fusion.1), kind=kCustom, calls=%fused_computation.6.clone | custom fusion | bytes 1064960 | tf_op jit(solution)/shard_map/jit(_take)/gather | solution.py:78
  81.9 14.9 %gather_fusion.5 = bf16[4096,64]{1,0:T(8,128)(2,1)} fusion(bf16[1024,64]{1,0:T(8,128)(2,1)S(1)} %get-tuple-element.453, s32[4096]{0:T(1024)S(1)} %broadcast_clamp_fusion.2), kind=kCustom, calls=%fused_computation.5.clone | custom fusion | bytes 1064960 | tf_op jit(solution)/shard_map/jit(_take)/gather | solution.py:78
  96.8 14.9 %gather_fusion.4 = bf16[4096,64]{1,0:T(8,128)(2,1)} fusion(bf16[1024,64]{1,0:T(8,128)(2,1)S(1)} %get-tuple-element.454, s32[4096]{0:T(1024)S(1)} %broadcast_clamp_fusion.3), kind=kCustom, calls=%fused_computation.4.clone | custom fusion | bytes 1064960 | tf_op jit(solution)/shard_map/jit(_take)/gather | solution.py:78
  111.7 14.9 %gather_fusion.3 = bf16[4096,64]{1,0:T(8,128)(2,1)} fusion(bf16[1024,64]{1,0:T(8,128)(2,1)S(1)} %get-tuple-element.455, s32[4096]{0:T(1024)S(1)} %broadcast_clamp_fusion.4), kind=kCustom, calls=%fused_computation.3.clone | custom fusion | bytes 1064960 | tf_op jit(solution)/shard_map/jit(_take)/gather | solution.py:78
  126.6 14.9 %gather_fusion.2 = bf16[4096,64]{1,0:T(8,128)(2,1)} fusion(bf16[1024,64]{1,0:T(8,128)(2,1)S(1)} %get-tuple-element.456, s32[4096]{0:T(1024)S(1)} %broadcast_clamp_fusion.5), kind=kCustom, calls=%fused_computation.2.clone | custom fusion | bytes 1064960 | tf_op jit(solution)/shard_map/jit(_take)/gather | solution.py:78
  141.5 14.9 %gather_fusion.1 = bf16[4096,64]{1,0:T(8,128)(2,1)} fusion(bf16[1024,64]{1,0:T(8,128)(2,1)S(1)} %get-tuple-element.457, s32[4096]{0:T(1024)S(1)} %broadcast_clamp_fusion.6), kind=kCustom, calls=%fused_computation.1.clone | custom fusion | bytes 1064960 | tf_op jit(solution)/shard_map/jit(_take)/gather | solution.py:78
  156.4 8.9 add_convert_fusion
  165.4 16.7 %copy.339 = bf16[1,4096,64]{2,0,1:T(2,128)(2,1)S(1)} copy(bf16[1,4096,64]{2,1,0:T(8,128)(2,1)S(1)} %add_convert_fusion) | data formatting | bytes 1048576 | tf_op jit(solution)/shard_map/convert_element_type | solution.py:82
  182.6 22.4 %reduce.51 = bf16[4096,64]{1,0:T(8,128)(2,1)S(1)} reduce(bf16[4096,1,64]{2,1,0:T(2,128)(2,1)S(1)} %bitcast.479, bf16[]{:T(256)} %broadcast.264), dimensions={1}, to_apply=%bitcast.393.reduce_sub_computation | reduce | bytes 1048578
  205.8 18.8 %all_to_all.44 = bf16[16,2,8192]{2,1,0:T(2,128)(2,1)S(1)} all-to-all(bf16[16,2,8192]{2,1,0:T(2,128)(2,1)S(1)} %reshape.934), channel_id=1, replica_groups=mesh['dp'=8,'ctx'=16] {'ctx'}, dimensions={0} | all-to-all | bytes 1048576 | tf_op jit(solution)/shard_map/all_to_all | solution.py:81
  230.3 4.6 fusion.102
  249.1 13.9 %collective-permute-done.1 = bf16[1,256,2048]{2,1,0:T(8,128)(2,1)} collective-permute-done((bf16[1,256,2048]{2,1,0:T(8,128)(2,1)}, bf16[1,256,2048]{2,1,0:T(8,128)(2,1)}, u32[]{:S(2)}, u32[]{:S(2)}) %collective-permute-start.1) | collective-permute-done | bytes 1048608 | tf_op jit(solution)/shard_map/ppermute | solution.py:14
  263.0 21.3 %collective-permute-done = bf16[1,256,2048]{2,1,0:T(8,128)(2,1)} collective-permute-done((bf16[1,256,2048]{2,1,0:T(8,128)(2,1)}, bf16[1,256,2048]{2,1,0:T(8,128)(2,1)}, u32[]{:S(2)}, u32[]{:S(2)}) %collective-permute-start) | collective-permute-done | bytes 1048608 | tf_op jit(solution)/shard_map/ppermute | solution.py:14
  288.9 4.0 copy.299
  292.9 4.0 copy.297
  296.9 4.7 copy.300
  301.5 46.4 %while.24 = (s32[]{:T(128)}, bf16[4,1,256,4,64]{2,4,3,1,0:T(8,128)(2,1)}, s32[4]{0:T(128)S(1)}, bf16[1,4,256,16,64]{2,1,4,3,0:T(4,128)(2,1)}, bf16[1,256,16,64]{...) while((s32[]{:T(128)}, ...), condition=%wide.region_10.12_spmd, body=%wide.region_4.11_spmd.sunk | while | flops 282916864 | bytes 16444675 | solution.py:129
  350.8 4.4 collective-permute-start.3
  357.0 4.0 collective-permute-done.4
  361.2 5.2 fusion.115
  378.4 5.6 fusion.120
  388.3 144.2 %while.25 = (s32[]{:T(128)}, bf16[4,1,256,4,64]{2,4,3,1,0:T(8,128)(2,1)}, f32[4,1,1024,4,64]{2,4,3,1,0:T(8,128)}, f32[4,1,1024,4,64]{2,4,3,1,0:T(8,128)}, s32[4]...) while((s32[]{:T(128)}, ...), condition=%wide.region_20.22_spmd, body=%wide.region_13.21_spmd.sunk | while | flops 716965888 | bytes 66809192 | solution.py:203
  406.4 7.1 fusion.265
  413.6 7.5 fusion.266
  442.3 7.1 fusion.265
  449.4 8.0 fusion.266
  478.9 7.1 fusion.265
  486.0 7.4 fusion.266
  514.8 7.1 fusion.265
  521.8 7.5 fusion.266
  532.4 5.6 reshape.813
  543.1 5.8 reshape.812
  575.5 7.6 pad_maximum_fusion.2
  584.3 7.3 pad_maximum_fusion.3
  591.6 5.5 collective-permute-start.9
  597.1 4.9 slice_bitcast_fusion
  602.2 35.2 %collective-permute-done.8 = bf16[1,256,2048]{1,0,2:T(2,128)(2,1)S(1)} collective-permute-done((bf16[1,256,2048]{1,0,2:T(2,128)(2,1)S(1)}, bf16[1,256,2048]{1,0,2:T(2,128)(2,1)S(1)}, u32[]{:S(2)}, u32[]{:S(2)}) %collective-permute-start.8) | collective-permute-done | bytes 1048608 | tf_op jit(solution)/shard_map/ppermute | solution.py:14
  639.6 19.2 %fusion.105 = bf16[1,256,2048]{1,0,2:T(2,128)(2,1)S(1)} fusion(bf16[1,256,2048]{1,0,2:T(2,128)(2,1)S(1)} %collective-permute-done.9, bf16[1,256,2048]{1,0,2:T(2,128)(2,1)S(1)} %collective-permute-done.8, f32[1,256,2048]{1,2,0:T(8,128)S(1)} %convert_element_type.227, f32[1,256,1024]{1,0,2:T(1,128)S(1)} %get-tuple-element.513, ...), kind=kLoop, calls=%fused_computation.149 | loop fusion | flops 3670016 | bytes 7340032 | tf_op jit(solution)/shard_map/convert_element_type | solution.py:221
  660.6 13.5 %all_to_all.45 = bf16[256,8,128]{0,2,1:T(8,128)(2,1)S(1)} all-to-all(bf16[256,8,128]{0,2,1:T(8,128)(2,1)S(1)} %multiply_convert_fusion.1), channel_id=1, replica_groups=mesh['dp'=8,'ctx'=16] {'dp'}, dimensions={1} | all-to-all | bytes 1048576 | tf_op jit(solution)/shard_map/all_to_all | solution.py:225
  679.2 8.6 all-to-all-done.2
  691.1 83.3 %all-gather.14.cloned.1.call-done = bf16[2048,3072]{0,1:T(8,128)(2,1)} async-done(((bf16[256,3072]{0,1:T(8,128)(2,1)}), bf16[2048,3072]{0,1:T(8,128)(2,1)}) %all-gather.14.cloned.1.call-update) | async-done | bytes 12582928 | tf_op jit(solution)/shard_map/all_gather | solution.py:226
  774.4 8.9 fusion.203
  787.4 4.8 multiply_reduce_fusion.1
  793.5 205.8 %all-gather.18.cloned.1.call-done = f32[2176,4096]{1,0:T(8,128)} async-done(((f32[136,4096]{1,0:T(8,128)}), f32[2176,4096]{1,0:T(8,128)}) %all-gather.18.cloned.1.call-update) | async-done | bytes 35651600 | tf_op jit(solution)/shard_map/all_gather | solution.py:244
  999.3 13.2 %reduce_sum.395 = f32[136,4096]{1,0:T(8,128)S(1)} reduce(f32[16,136,4096]{2,1,0:T(8,128)} %bitcast.475, f32[]{:T(128)} %constant.63.clone.1), dimensions={0}, to_apply=%region_54.56 | reduce | flops 8355840 | bytes 37879812 | tf_op jit(solution)/shard_map/reduce_sum | solution.py:244
  (272 shorter events, 233.6 us)
Async XLA Ops:
  7.2 237.8 %copy-start = (s32[16,1]{0,1:T(1,128)S(1)}, s32[16,1]{0,1:T(1,128)}, u32[]{:S(2)}) copy-start(s32[16,1]{0,1:T(1,128)} %param.24) | copy-start | bytes 196
  7.2 31.0 %all-gather.8.cloned.1.call-start = ((), (), s32[]{:S(2)}) async-start(), calls=%async_computation.3 | async-start | bytes 2359296 | tf_op jit(solution)/shard_map/all_gather | solution.py:75
  9.0 220.7 %all-gather.10.cloned.1.call-start = ((), (), s32[]{:S(2)}) async-start(), calls=%async_computation.4 | async-start | bytes 7077888 | tf_op jit(solution)/shard_map/all_gather | solution.py:85
  9.8 338.2 %all-gather.12.cloned.1.call-start = ((), (), s32[]{:S(2)}) async-start(), calls=%async_computation.5 | async-start | bytes 2359296 | tf_op jit(solution)/shard_map/all_gather | solution.py:86
  141.5 14.9 %copy-start.12 = (bf16[4096,64]{1,0:T(8,128)(2,1)S(1)}, bf16[4096,64]{1,0:T(8,128)(2,1)}, u32[]{:S(2)}) copy-start(bf16[4096,64]{1,0:T(8,128)(2,1)} %gather_fusion.7) | copy-start | bytes 1572868
  228.1 2.2 copy-start.19
  229.2 5.7 copy-start.8
  229.6 118.3 %copy-start.6 = (f32[256,1024]{1,0:T(8,128)}, f32[256,1024]{1,0:T(8,128)S(1)}, u32[]{:S(2)}) copy-start(f32[256,1024]{1,0:T(8,128)S(1)} %copy.302) | copy-start | bytes 3145732
  229.6 0.6 copy-start.21
  229.6 16.6 %copy-start.23 = (s32[16,2]{0,1:T(2,128)S(1)}, s32[16,2]{0,1:T(2,128)}, u32[]{:S(2)}) copy-start(s32[16,2]{0,1:T(2,128)} %param.23) | copy-start | bytes 388
  229.7 17.3 %copy-start.17 = (f32[31,1024]{1,0:T(8,128)S(1)}, f32[31,1024]{1,0:T(8,128)}, u32[]{:S(2)}) copy-start(f32[31,1024]{1,0:T(8,128)} %param.22) | copy-start | bytes 380932
  234.9 1.5 copy-start.14
  236.4 26.6 %collective-permute-start.1 = (bf16[1,256,2048]{2,1,0:T(8,128)(2,1)}, bf16[1,256,2048]{2,1,0:T(8,128)(2,1)}, u32[]{:S(2)}, u32[]{:S(2)}) collective-permute-start(bf16[1,256,2048]{2,1,0:T(8,128)(2,1)} %get-tuple-element.459), channel_id=1, source_target_pairs={{0,2},{1,3},{2,4},{3,5},{4,6},{5,7},{6,8},{7,9},{8,10},{9,11},{10,... | collective-permute-start | bytes 3145736 | tf_op jit(solution)/shard_map/ppermute | solution.py:14
  240.1 44.2 %collective-permute-start = (bf16[1,256,2048]{2,1,0:T(8,128)(2,1)}, bf16[1,256,2048]{2,1,0:T(8,128)(2,1)}, u32[]{:S(2)}, u32[]{:S(2)}) collective-permute-start(bf16[1,256,2048]{2,1,0:T(8,128)(2,1)} %get-tuple-element.459), channel_id=1, source_target_pairs={{0,1},{1,2},{2,3},{3,4},{4,5},{5,6},{6,7},{7,8},{8,9},{9,10},{10,1... | collective-permute-start | bytes 3145736 | tf_op jit(solution)/shard_map/ppermute | solution.py:14
  243.6 40.7 %collective-permute-start.2 = (bf16[1,256,2048]{2,1,0:T(8,128)(2,1)}, bf16[1,256,2048]{2,1,0:T(8,128)(2,1)}, u32[]{:S(2)}, u32[]{:S(2)}) collective-permute-start(bf16[1,256,2048]{2,1,0:T(8,128)(2,1)} %get-tuple-element.459), channel_id=1, source_target_pairs={{1,0},{2,1},{3,2},{4,3},{5,4},{6,5},{7,6},{8,7},{9,8},{10,9},{11,1... | collective-permute-start | bytes 3145736 | tf_op jit(solution)/shard_map/ppermute | solution.py:14
  244.9 433.3 %all-reduce.3.cloned.1.call-start = ((), (), s32[]{:S(2)}) async-start(), calls=%async_computation.8 | async-start | bytes 262144 | tf_op jit(solution)/shard_map/psum | solution.py:160
  347.9 2.7 copy-start.18
  347.9 13.3 %copy-start.13 = (bf16[1,256,1024]{2,1,0:T(8,128)(2,1)S(1)}, bf16[1,256,1024]{2,1,0:T(8,128)(2,1)}, u32[]{:S(2)}) copy-start(bf16[1,256,1024]{2,1,0:T(8,128)(2,1)} %param.25) | copy-start | bytes 1572868
  350.6 33.4 %copy-start.4 = (bf16[256,1024]{1,0:T(8,128)(2,1)}, bf16[256,1024]{1,0:T(8,128)(2,1)S(1)}, u32[]{:S(2)}) copy-start(bf16[256,1024]{1,0:T(8,128)(2,1)S(1)} %get-tuple-element.510) | copy-start | bytes 1572868
  350.8 6.2 collective-permute-start.3
  355.2 5.8 collective-permute-start.4
  369.0 9.2 collective-permute-start.5
  372.3 5.8 collective-permute-start.6
  378.1 310.0 %all-gather.16.cloned.1.call-start = ((), (), s32[]{:S(2)}) async-start(), calls=%async_computation.7 | async-start | bytes 4718592 | tf_op jit(solution)/shard_map/all_gather | solution.py:171
  384.5 3.5 copy-start.10
  388.0 386.4 %all-gather.14.cloned.1.call-start = ((), (), s32[]{:S(2)}) async-start(), calls=%async_computation.6 | async-start | bytes 14155776 | tf_op jit(solution)/shard_map/all_gather | solution.py:226
  396.5 6.3 copy-start.3
  401.2 1.0 copy-start.2
  432.4 6.3 copy-start.3
  437.1 1.0 copy-start.2
  469.0 6.3 copy-start.3
  473.7 1.0 copy-start.2
  504.8 6.3 copy-start.3
  509.5 1.0 copy-start.2
  574.2 27.9 %collective-permute-start.7 = (bf16[1,256,2048]{1,2,0:T(8,128)(2,1)S(1)}, bf16[1,256,2048]{1,2,0:T(8,128)(2,1)S(1)}, u32[]{:S(2)}, u32[]{:S(2)}) collective-permute-start(bf16[1,256,2048]{1,2,0:T(8,128)(2,1)S(1)} %pad_maximum_fusion.5), channel_id=1, source_target_pairs={{1,0},{2,1},{3,2},{4,3},{5,4},{6,5},{7,6},{8,7},{9,8},{10,9},{11,1... | collective-permute-start | bytes 3145736 | tf_op jit(solution)/shard_map/ppermute | solution.py:14
  583.0 54.3 %collective-permute-start.8 = (bf16[1,256,2048]{1,0,2:T(2,128)(2,1)S(1)}, bf16[1,256,2048]{1,0,2:T(2,128)(2,1)S(1)}, u32[]{:S(2)}, u32[]{:S(2)}) collective-permute-start(bf16[1,256,2048]{1,0,2:T(2,128)(2,1)S(1)} %pad_maximum_fusion.2), channel_id=1, source_target_pairs={{2,0},{3,1},{4,2},{5,3},{6,4},{7,5},{8,6},{9,7},{10,8},{11,9},{12,... | collective-permute-start | bytes 3145736 | tf_op jit(solution)/shard_map/ppermute | solution.py:14
  591.6 48.0 %collective-permute-start.9 = (bf16[1,256,2048]{1,0,2:T(2,128)(2,1)S(1)}, bf16[1,256,2048]{1,0,2:T(2,128)(2,1)S(1)}, u32[]{:S(2)}, u32[]{:S(2)}) collective-permute-start(bf16[1,256,2048]{1,0,2:T(2,128)(2,1)S(1)} %pad_maximum_fusion.3), channel_id=1, source_target_pairs={{0,1},{1,2},{2,3},{3,4},{4,5},{5,6},{6,7},{7,8},{8,9},{9,10},{10,1... | collective-permute-start | bytes 3145736 | tf_op jit(solution)/shard_map/ppermute | solution.py:14
  639.6 19.4 %copy-start.15 = (bf16[4,1,256,4,64]{2,4,3,1,0:T(8,128)(2,1)S(1)}, bf16[4,1,256,4,64]{2,4,3,1,0:T(8,128)(2,1)}, u32[]{:S(2)}) copy-start(bf16[4,1,256,4,64]{2,4,3,1,0:T(8,128)(2,1)} %get-tuple-element.118) | copy-start | bytes 1572868
  658.8 1.5 copy-start.9
  658.8 1.5 copy-start.20
  658.8 1.5 copy-start.22
  674.1 13.8 %all-to-all-start.2 = ((bf16[256,8,128]{0,2,1:T(8,128)(2,1)}), bf16[256,8,128]{0,2,1:T(8,128)(2,1)S(1)}, u32[]{:S(2)}, u32[]{:S(2)}) async-start(bf16[256,8,128]{0,2,1:T(8,128)(2,1)} %bitcast.135), calls=%async_computation.2 | async-start | bytes 1048576 | tf_op jit(solution)/shard_map/all_to_all | solution.py:170
  677.6 321.8 %all-gather.18.cloned.1.call-start = ((), (), s32[]{:S(2)}) async-start(), calls=%async_computation.9 | async-start | bytes 37879808 | tf_op jit(solution)/shard_map/all_gather | solution.py:244
  783.4 1.6 copy-start.5
  783.4 4.1 copy-start.7
  785.0 2.5 copy-start.16
  787.4 4.8 copy-start.11
  999.3 16.0 %copy-start.1 = (s32[16,1]{0,1:T(1,128)S(1)}, s32[16,1]{0,1:T(1,128)}, u32[]{:S(2)}) copy-start(s32[16,1]{0,1:T(1,128)} %param.24) | copy-start | bytes 196
Sparse Core Ops, SparseCore 0:
  10.3 27.8 all-gather.7
  39.9 41.4 all-gather.9
  245.0 24.3 all-gather.11
  378.2 62.7 all-reduce.2
  442.7 31.2 all-gather.15
  660.5 113.9 all-gather.13
  785.1 214.1 all-gather.17
